TPU v7x, 32 devices: a whole 2x2x4 slice. The times are simulated.
32 devices in a mesh: rep: 2 (over x), member: 4 (over y, core), tp: 4 (over z).
Axes of the slice: x: 2, y: 2, z: 4, core: 2. Of those that a mesh axis runs over, the one named last changes fastest.
Arguments:
- states: bfloat16 [4096, 1024], P(('rep', 'member', 'tp')), parts along dimension 0, may hold values from -6 to 6
- member_of: int32 [4096, 1], P(('rep', 'member', 'tp')), parts along dimension 0, may hold values from 0 to 1; in each aligned block of 128 rows (0 to 127, 128 to 255, ...) at most 128 rows name the same one
- place: int32 [4096], P(('rep', 'member', 'tp')), parts along dimension 0, may hold values from 0 to 2047, as said below
- norm_gain: float32 [2, 1024], replicated, may hold values from 0.5 to 2
- w_up: bfloat16 [4, 1024, 2048], P('member', None, 'tp'), may hold values from -0.1875 to 0.1875
- w_down: bfloat16 [4, 2048, 1024], P('member', 'tp'), may hold values from -0.09375 to 0.09375
- policy_gain: float32 [1024], replicated, may hold values from 0.5 to 2
- w_policy: bfloat16 [1024, 128], replicated, may hold values from -0.1875 to 0.1875
Outputs:
- imagined: bfloat16 [4096, 1024], P(('rep', 'member', 'tp')), parts along dimension 0
- action: bfloat16 [4096, 128], P(('rep', 'member', 'tp')), parts along dimension 0
There are 2 independent parts, one for each index of `rep`. A program takes and returns all parts, laid end to end along the dimension named above; an argument that names none is the same for every part. Nothing has to cross between parts.
Inputs may be any that keep to these rules, and one draw needn't show every extreme that they name: `member_of`: at most 128 of the rows of one device name any one member, and that count is reached on some device. `place`: A permutation of the 2048 learner positions; learner device k holds positions k * 128 to (k + 1) * 128 - 1, and the rows of each device go exactly 8 to every learner device.
All inputs are finite; a program needn't handle non-finite values.
Results may differ from a plain program's by a relative error of at most 0.0069.
Values may be sent and summed in bfloat16 or wider, within the bound.
No kernel may reach another device: no remote copies, remote signals or barrier semaphores. Data moves between devices by JAX's collectives and lax.ppermute only.
A program may use at most 128 MiB of HBM per device.

v0:
```python
import jax
import jax.numpy as jnp
from jax import lax
from jax.sharding import PartitionSpec as P

PARTIAL_DTYPE = jnp.bfloat16


def from_partner(value, axis, distance):
    return lax.ppermute(value, axis, [(i, i ^ 1 << distance) for i in range(lax.axis_size(axis))])


def from_chip_behind(value, axis, chips_back):
    size = lax.axis_size(axis)
    return lax.ppermute(value, axis, [(i, (i + 2 * chips_back) % size) for i in range(size)])


def swap_parts(value):
    n_rep = lax.axis_size("rep")
    return [value] + [
        lax.ppermute(value, "rep", [(i, (i + step) % n_rep) for i in range(n_rep)])
        for step in range(1, n_rep)
    ]


def fetch_shared(up, down, chips_back):
    n_rep = lax.axis_size("rep")
    share = up.shape[1] // n_rep
    rep_here = lax.axis_index("rep")
    got_up = from_chip_behind(
        lax.dynamic_slice_in_dim(up, rep_here * share, share, axis=1), "member", chips_back
    )
    got_up, down = lax.optimization_barrier((got_up, down))
    got_down = from_chip_behind(
        lax.dynamic_slice_in_dim(down, rep_here * share, share, axis=0), "member", chips_back
    )
    up_parts = swap_parts(got_up)
    down_parts = swap_parts(got_down)
    partner_up = [from_partner(part, "member", 0) for part in up_parts]
    partner_down = [from_partner(part, "member", 0) for part in down_parts]
    return (up_parts + partner_up, down_parts + partner_down)


def rms_scale(values, gain):
    mean_square = jnp.mean(values * values, axis=-1, keepdims=True)
    return values * lax.rsqrt(mean_square + 1e-06) * gain


def running_rank(member_hits):
    return jnp.sum((jnp.cumsum(member_hits, axis=0) - member_hits) * member_hits, axis=1)


def local(states, member_of, place, norm_gain, w_up, w_down, policy_gain, w_policy):
    n_member = lax.axis_size("member")
    n_tp = lax.axis_size("tp")
    n_dev = n_member * n_tp
    member_total = n_member // 2
    rows_here = states.shape[0]
    feature_width = states.shape[1]
    own_member = lax.axis_index("member") // 2
    own_block = (own_member, w_up[0], w_down[0])
    fetched = [
        ((own_member - back + member_total) % member_total, *fetch_shared(w_up[0], w_down[0], back))
        for back in range(1, member_total)
    ]
    per_learner = rows_here // n_dev
    learner = place // rows_here
    learner_hits = (learner[:, None] == jnp.arange(n_dev, dtype=jnp.int32)[None, :]).astype(
        jnp.int32
    )
    lane_index = learner * per_learner + running_rank(learner_hits)
    placer = jnp.arange(rows_here, dtype=jnp.int32)[:, None] == lane_index[None, :]
    states = jnp.dot(
        placer.astype(jnp.bfloat16), states, preferred_element_type=jnp.float32
    ).astype(jnp.bfloat16)
    member = jnp.sum(placer.astype(jnp.int32) * member_of[:, 0][None, :], axis=1)
    packed_spot = jnp.sum(placer.astype(jnp.int32) * (place % rows_here)[None, :], axis=1)
    gain_rows = jnp.take(norm_gain, member, axis=0)
    normed = rms_scale(states.astype(jnp.float32), gain_rows).astype(jnp.bfloat16)
    member_lanes = jnp.where(
        jnp.arange(128, dtype=jnp.int32)[None, :] == 0, member[:, None], 0
    ).astype(jnp.bfloat16)
    gathered = lax.all_gather(
        jnp.concatenate([normed, member_lanes], axis=1), "tp", axis=0, tiled=True
    )
    gathered_rows = gathered[:, :feature_width]
    gathered_member = gathered[:, feature_width].astype(jnp.int32)

    def apply_block(block_member, up_here, down_here):
        keep = (gathered_member == block_member).astype(jnp.bfloat16)[:, None]
        hidden = (
            jax.nn.gelu(jnp.dot(gathered_rows, up_here, preferred_element_type=jnp.float32)).astype(
                jnp.bfloat16
            )
            * keep
        )
        return jnp.dot(hidden, down_here, preferred_element_type=jnp.float32)

    def apply_pair(block_member, up_here, down_here):
        both_up = jnp.concatenate([up_here, from_partner(up_here, "member", 0)], axis=1)
        both_down = jnp.concatenate([down_here, from_partner(down_here, "member", 0)], axis=0)
        return apply_block(block_member, both_up, both_down)

    terms = [apply_pair(*own_block)]
    for block_member, up_here, down_here in fetched:
        terms, up_here, down_here = lax.optimization_barrier((terms, up_here, down_here))
        terms = terms + [
            apply_block(
                block_member, jnp.concatenate(up_here, axis=1), jnp.concatenate(down_here, axis=0)
            )
        ]
    tp_here = lax.axis_index("tp")
    by_target = [term.reshape(n_tp, rows_here, feature_width) for term in terms]

    def slice_for(target):
        pieces = [lax.dynamic_index_in_dim(term, target, 0, keepdims=False) for term in by_target]
        total = pieces[0]
        for piece in pieces[1:]:
            total = total + piece
        return total

    change = slice_for(tp_here)
    for shift in range(1, n_tp):
        change = change + lax.ppermute(
            slice_for((tp_here + shift) % n_tp).astype(PARTIAL_DTYPE),
            "tp",
            [(i, (i + shift) % n_tp) for i in range(n_tp)],
        ).astype(jnp.float32)
    packed = (states.astype(jnp.float32) + change).astype(jnp.bfloat16)
    spot_lanes = jnp.where(
        jnp.arange(128, dtype=jnp.int32)[None, :] == 0, packed_spot[:, None], 0
    ).astype(jnp.bfloat16)
    arrivals = lax.all_to_all(
        jnp.concatenate([packed, spot_lanes], axis=1).reshape(
            n_dev, per_learner, feature_width + 128
        ),
        ("member", "tp"),
        split_axis=0,
        concat_axis=0,
        tiled=True,
    )
    arrivals = arrivals.reshape(n_dev * per_learner, feature_width + 128)
    arrival_spots = arrivals[:, feature_width].astype(jnp.int32)
    settle = (jnp.arange(rows_here, dtype=jnp.int32)[:, None] == arrival_spots[None, :]).astype(
        jnp.bfloat16
    )
    imagined = jnp.dot(
        settle, arrivals[:, :feature_width], preferred_element_type=jnp.float32
    ).astype(jnp.bfloat16)
    policy_normed = rms_scale(imagined.astype(jnp.float32), policy_gain).astype(jnp.bfloat16)
    action = jnp.tanh(jnp.dot(policy_normed, w_policy, preferred_element_type=jnp.float32)).astype(
        jnp.bfloat16
    )
    return (imagined, action)


def solution(mesh):
    in_specs = (
        P(("rep", "member", "tp"), None),
        P(("rep", "member", "tp"), None),
        P(("rep", "member", "tp")),
        P(),
        P("member", None, "tp"),
        P("member", "tp", None),
        P(),
        P(),
    )
    out_specs = (P(("rep", "member", "tp"), None), P(("rep", "member", "tp"), None))
    return jax.shard_map(local, mesh=mesh, in_specs=in_specs, out_specs=out_specs, check_vma=False)
```

profile of v0, /device:TPU:0, one launch (start us, length us, event | category | flops | bytes accessed | tf_op | source)
XLA Modules:
  0.0 118.7 jit_solution(594228416031735746)
XLA Ops:
  7.2 0.7 and_select_fusion
  8.0 0.2 reduce_window_sum.11
  8.2 0.2 select_reduce_fusion.2
  8.4 0.8 select_reduce_fusion.1
  9.2 0.3 multiply_reduce_fusion
  9.5 0.1 select_convert_fusion.1
  9.6 0.8 gather_fusion
  10.4 0.1 multiply_convert_fusion
  10.6 0.8 pad_maximum_fusion
  11.4 0.4 copy-done.3
  11.8 3.0 %collective-permute-start.2 = (bf16[1024,256]{1,0:T(8,128)(2,1)S(1)}, bf16[1024,256]{1,0:T(8,128)(2,1)S(1)}, u32[]{:S(2)}, u32[]{:S(2)}) collective-permute-start(bf16[1024,256]{1,0:T(8,128)(2,1)S(1)} %dynamic-slice_bitcast_fusion), channel_id=1, source_target_pairs={{0,8},{4,12},{8,0},{12,4},{1,9},{5,13},{9,1},{13,5},{2,10},{6,14},... | collective-permute-start | bytes 1572872 | tf_op jit(solution)/shard_map/ppermute | solution.py:15
  14.8 11.9 %collective-permute-done.2 = bf16[1024,256]{1,0:T(8,128)(2,1)S(1)} collective-permute-done((bf16[1024,256]{1,0:T(8,128)(2,1)S(1)}, bf16[1024,256]{1,0:T(8,128)(2,1)S(1)}, u32[]{:S(2)}, u32[]{:S(2)}) %collective-permute-start.2) | collective-permute-done | bytes 524320 | tf_op jit(solution)/shard_map/ppermute | solution.py:15
  26.8 1.8 %collective-permute-start.6 = (bf16[256,1024]{1,0:T(8,128)(2,1)S(1)}, bf16[256,1024]{1,0:T(8,128)(2,1)}, u32[]{:S(2)}, u32[]{:S(2)}) collective-permute-start(bf16[256,1024]{1,0:T(8,128)(2,1)S(1)} %constant_dynamic-slice_fusion), channel_id=1, source_target_pairs={{0,8},{4,12},{8,0},{12,4},{1,9},{5,13},{9,1},{13,5},{2,10},{6,14},... | collective-permute-start | bytes 1572872 | tf_op jit(solution)/shard_map/ppermute | solution.py:15
  28.6 1.5 %collective-permute-start.3 = (bf16[1024,256]{1,0:T(8,128)(2,1)S(1)}, bf16[1024,256]{1,0:T(8,128)(2,1)}, u32[]{:S(2)}, u32[]{:S(2)}) collective-permute-start(bf16[1024,256]{1,0:T(8,128)(2,1)S(1)} %collective-permute-done.2), channel_id=1, source_target_pairs={{0,16},{16,0},{1,17},{17,1},{2,18},{18,2},{3,19},{19,3},{4,20},{20... | collective-permute-start | bytes 1572872 | tf_op jit(solution)/shard_map/ppermute | solution.py:21
  30.1 10.1 %collective-permute-done.6 = bf16[256,1024]{1,0:T(8,128)(2,1)} collective-permute-done((bf16[256,1024]{1,0:T(8,128)(2,1)S(1)}, bf16[256,1024]{1,0:T(8,128)(2,1)}, u32[]{:S(2)}, u32[]{:S(2)}) %collective-permute-start.6) | collective-permute-done | bytes 524320 | tf_op jit(solution)/shard_map/ppermute | solution.py:15
  40.2 1.4 %collective-permute-start.7 = (bf16[256,1024]{1,0:T(8,128)(2,1)}, bf16[256,1024]{1,0:T(8,128)(2,1)}, u32[]{:S(2)}, u32[]{:S(2)}) collective-permute-start(bf16[256,1024]{1,0:T(8,128)(2,1)} %collective-permute-done.6), channel_id=1, source_target_pairs={{0,16},{16,0},{1,17},{17,1},{2,18},{18,2},{3,19},{19,3},{4,20},{20... | collective-permute-start | bytes 1572872 | tf_op jit(solution)/shard_map/ppermute | solution.py:21
  41.6 3.1 %all-gather.2.cloned.1.call-done = bf16[512,1152]{1,0:T(8,128)(2,1)} async-done(((bf16[128,1152]{1,0:T(8,128)(2,1)}), bf16[512,1152]{1,0:T(8,128)(2,1)}) %all-gather.2.cloned.1.call-update) | async-done | bytes 1179664 | tf_op jit(solution)/shard_map/all_gather | solution.py:83
  44.7 1.1 fusion.84
  45.8 0.5 collective-permute-start.5
  46.3 7.9 %collective-permute-done.7 = bf16[256,1024]{1,0:T(8,128)(2,1)} collective-permute-done((bf16[256,1024]{1,0:T(8,128)(2,1)}, bf16[256,1024]{1,0:T(8,128)(2,1)}, u32[]{:S(2)}, u32[]{:S(2)}) %collective-permute-start.7) | collective-permute-done | bytes 524320 | tf_op jit(solution)/shard_map/ppermute | solution.py:21
  54.3 4.9 %fusion.20 = f32[512,1024]{1,0:T(8,128)S(1)} fusion(bf16[512,1024]{1,0:T(8,128)(2,1)} %collective-permute-done.1, bf16[512,1024]{1,0:T(8,128)(2,1)} %bitcast.38, bf16[1024,512]{1,0:T(8,128)(2,1)} %collective-permute-done, bf16[1024,512]{1,0:T(8,128)(2,1)} %bitcast.41, bf16[512,1152]{1,0:T(8,128)(2,1)} %all-gather.2.cloned.1.call-done, ...), kind=kOutput, calls=%fused_computation.23 | convolution fusion | flops 2161115136 | bytes 7341056 | tf_op jit(solution)/shard_map/dot_general | solution.py:97
  59.2 6.0 %fusion.32 = f32[512,1024]{1,0:T(8,128)} fusion(bf16[256,1024]{1,0:T(8,128)(2,1)} %collective-permute-done.9, bf16[256,1024]{1,0:T(8,128)(2,1)} %collective-permute-done.8, bf16[256,1024]{1,0:T(8,128)(2,1)} %collective-permute-done.7, bf16[256,1024]{1,0:T(8,128)(2,1)} %collective-permute-done.6, bf16[1024,256]{1,0:T(8,128)(2,1)} %collective-permute-done.5, ...), kind=kOutput, calls=%fused_computation.35 | convolution fusion | flops 2169503744 | bytes 7341056 | tf_op jit(solution)/shard_map/dot_general | solution.py:97
  65.3 2.3 %fusion.75 = (bf16[128,1024]{1,0:T(8,128)(2,1)S(1)}, bf16[128,1024]{1,0:T(8,128)(2,1)}, bf16[128,1024]{1,0:T(8,128)(2,1)S(1)}) fusion(f32[4,128,1024]{2,1,0:T(8,128)} %bitcast.34, s32[]{:T(128)S(6)} %select_n.91, f32[4,128,1024]{2,1,0:T(8,128)S(1)} %bitcast.32, s32[]{:T(128)S(6)} %select_n.95, s32[]{:T(128)S(6)} %select_n.93), kind=kLoop, calls=%fused_computation.77 | loop fusion | flops 786432 | bytes 3932172 | tf_op jit(solution)/shard_map/convert_element_type | solution.py:125
  67.5 3.6 %collective-permute-start.12 = (bf16[128,1024]{1,0:T(8,128)(2,1)}, bf16[128,1024]{1,0:T(8,128)(2,1)}, u32[]{:S(2)}, u32[]{:S(2)}) collective-permute-start(bf16[128,1024]{1,0:T(8,128)(2,1)} %get-tuple-element.29), channel_id=1, source_target_pairs={{0,3},{1,0},{2,1},{3,2},{4,7},{5,4},{6,5},{7,6},{8,11},{9,8},{10,9... | collective-permute-start | bytes 786440 | tf_op jit(solution)/shard_map/ppermute | solution.py:124
  71.1 1.0 collective-permute-start.10
  72.2 6.0 %collective-permute-done.12 = bf16[128,1024]{1,0:T(8,128)(2,1)} collective-permute-done((bf16[128,1024]{1,0:T(8,128)(2,1)}, bf16[128,1024]{1,0:T(8,128)(2,1)}, u32[]{:S(2)}, u32[]{:S(2)}) %collective-permute-start.12) | collective-permute-done | bytes 262176 | tf_op jit(solution)/shard_map/ppermute | solution.py:124
  78.2 16.3 %collective-permute-done.11 = bf16[128,1024]{1,0:T(8,128)(2,1)} collective-permute-done((bf16[128,1024]{1,0:T(8,128)(2,1)S(1)}, bf16[128,1024]{1,0:T(8,128)(2,1)}, u32[]{:S(2)}, u32[]{:S(2)}) %collective-permute-start.11) | collective-permute-done | bytes 262176 | tf_op jit(solution)/shard_map/ppermute | solution.py:124
  94.5 1.5 %fusion.72 = bf16[128,1024]{1,0:T(8,128)(2,1)S(1)} fusion(f32[128,1024]{1,0:T(8,128)S(1)} %get-tuple-element.36, bf16[128,1024]{1,0:T(8,128)(2,1)} %collective-permute-done.12, bf16[128,1024]{1,0:T(8,128)(2,1)} %collective-permute-done.11, bf16[128,1024]{1,0:T(8,128)(2,1)} %collective-permute-done.10, f32[4,128,1024]{2,1,0:T(8,128)} %bitcast.35, ...), kind=kLoop, calls=%fused_computation.64 | loop fusion | flops 1179648 | bytes 2621444 | tf_op jit(solution)/shard_map/convert_element_type | solution.py:129
  96.0 14.5 %all_to_all.5 = bf16[16,8,1152]{2,1,0:T(8,128)(2,1)S(1)} all-to-all(bf16[16,8,1152]{2,1,0:T(8,128)(2,1)S(1)} %maximum_bitcast_fusion), channel_id=1, replica_groups=mesh['rep'=2,'member'=4,'tp'=4] {'member','tp'}, dimensions={0} | all-to-all | bytes 589824 | tf_op jit(solution)/shard_map/all_to_all | solution.py:133
  110.5 0.1 convert_reduce_fusion
  110.6 0.3 fusion.66
  111.0 0.9 fusion.41
  (39 shorter events, 0.4 us)
Async XLA Ops:
  7.2 2.0 %copy-start = (bf16[128,1024]{1,0:T(8,128)(2,1)S(1)}, bf16[128,1024]{1,0:T(8,128)(2,1)}, u32[]{:S(2)}) copy-start(bf16[128,1024]{1,0:T(8,128)(2,1)} %param.8) | copy-start | bytes 786436
  7.2 2.4 %copy-start.1 = (f32[2,1024]{1,0:T(2,128)S(1)}, f32[2,1024]{1,0:T(2,128)}, u32[]{:S(2)}) copy-start(f32[2,1024]{1,0:T(2,128)} %param.11) | copy-start | bytes 24580
  7.2 37.5 %all-gather.2.cloned.1.call-start = ((), (), s32[]{:S(2)}) async-start(), calls=%async_computation.1 | async-start | bytes 1474560 | tf_op jit(solution)/shard_map/all_gather | solution.py:83
  10.4 1.3 %copy-start.3 = (bf16[1,1024,512]{2,1,0:T(8,128)(2,1)S(1)}, bf16[1,1024,512]{2,1,0:T(8,128)(2,1)}, u32[]{:S(2)}) copy-start(bf16[1,1024,512]{2,1,0:T(8,128)(2,1)} %param.12) | copy-start | bytes 3145732
  10.4 4.4 %copy-start.2 = (bf16[1,512,1024]{2,1,0:T(8,128)(2,1)S(1)}, bf16[1,512,1024]{2,1,0:T(8,128)(2,1)}, u32[]{:S(2)}) copy-start(bf16[1,512,1024]{2,1,0:T(8,128)(2,1)} %param.13) | copy-start | bytes 3145732
  11.8 15.0 %collective-permute-start.2 = (bf16[1024,256]{1,0:T(8,128)(2,1)S(1)}, bf16[1024,256]{1,0:T(8,128)(2,1)S(1)}, u32[]{:S(2)}, u32[]{:S(2)}) collective-permute-start(bf16[1024,256]{1,0:T(8,128)(2,1)S(1)} %dynamic-slice_bitcast_fusion), channel_id=1, source_target_pairs={{0,8},{4,12},{8,0},{12,4},{1,9},{5,13},{9,1},{13,5},{2,10},{6,14},... | collective-permute-start | bytes 1572872 | tf_op jit(solution)/shard_map/ppermute | solution.py:15
  14.8 30.9 %collective-permute-start.1 = (bf16[512,1024]{1,0:T(8,128)(2,1)S(1)}, bf16[512,1024]{1,0:T(8,128)(2,1)}, u32[]{:S(2)}, u32[]{:S(2)}) collective-permute-start(bf16[512,1024]{1,0:T(8,128)(2,1)S(1)} %bitcast.39), channel_id=1, source_target_pairs={{0,4},{4,0},{8,12},{12,8},{1,5},{5,1},{9,13},{13,9},{2,6},{6,2},{1... | collective-permute-start | bytes 3145736 | tf_op jit(solution)/shard_map/ppermute | solution.py:10
  26.8 13.4 %collective-permute-start.6 = (bf16[256,1024]{1,0:T(8,128)(2,1)S(1)}, bf16[256,1024]{1,0:T(8,128)(2,1)}, u32[]{:S(2)}, u32[]{:S(2)}) collective-permute-start(bf16[256,1024]{1,0:T(8,128)(2,1)S(1)} %constant_dynamic-slice_fusion), channel_id=1, source_target_pairs={{0,8},{4,12},{8,0},{12,4},{1,9},{5,13},{9,1},{13,5},{2,10},{6,14},... | collective-permute-start | bytes 1572872 | tf_op jit(solution)/shard_map/ppermute | solution.py:15
  28.6 25.7 %collective-permute-start = (bf16[1024,512]{1,0:T(8,128)(2,1)S(1)}, bf16[1024,512]{1,0:T(8,128)(2,1)}, u32[]{:S(2)}, u32[]{:S(2)}) collective-permute-start(bf16[1024,512]{1,0:T(8,128)(2,1)S(1)} %bitcast.42), channel_id=1, source_target_pairs={{0,4},{4,0},{8,12},{12,8},{1,5},{5,1},{9,13},{13,9},{2,6},{6,2},{1... | collective-permute-start | bytes 3145736 | tf_op jit(solution)/shard_map/ppermute | solution.py:10
  28.6 17.2 %collective-permute-start.3 = (bf16[1024,256]{1,0:T(8,128)(2,1)S(1)}, bf16[1024,256]{1,0:T(8,128)(2,1)}, u32[]{:S(2)}, u32[]{:S(2)}) collective-permute-start(bf16[1024,256]{1,0:T(8,128)(2,1)S(1)} %collective-permute-done.2), channel_id=1, source_target_pairs={{0,16},{16,0},{1,17},{17,1},{2,18},{18,2},{3,19},{19,3},{4,20},{20... | collective-permute-start | bytes 1572872 | tf_op jit(solution)/shard_map/ppermute | solution.py:21
  40.2 14.1 %collective-permute-start.7 = (bf16[256,1024]{1,0:T(8,128)(2,1)}, bf16[256,1024]{1,0:T(8,128)(2,1)}, u32[]{:S(2)}, u32[]{:S(2)}) collective-permute-start(bf16[256,1024]{1,0:T(8,128)(2,1)} %collective-permute-done.6), channel_id=1, source_target_pairs={{0,16},{16,0},{1,17},{17,1},{2,18},{18,2},{3,19},{19,3},{4,20},{20... | collective-permute-start | bytes 1572872 | tf_op jit(solution)/shard_map/ppermute | solution.py:21
  41.6 17.6 %collective-permute-start.4 = (bf16[1024,256]{1,0:T(8,128)(2,1)S(1)}, bf16[1024,256]{1,0:T(8,128)(2,1)}, u32[]{:S(2)}, u32[]{:S(2)}) collective-permute-start(bf16[1024,256]{1,0:T(8,128)(2,1)S(1)} %collective-permute-done.2), channel_id=1, source_target_pairs={{0,4},{4,0},{8,12},{12,8},{1,5},{5,1},{9,13},{13,9},{2,6},{6,2},{1... | collective-permute-start | bytes 1572872 | tf_op jit(solution)/shard_map/ppermute | solution.py:10
  45.8 13.5 %collective-permute-start.8 = (bf16[256,1024]{1,0:T(8,128)(2,1)}, bf16[256,1024]{1,0:T(8,128)(2,1)}, u32[]{:S(2)}, u32[]{:S(2)}) collective-permute-start(bf16[256,1024]{1,0:T(8,128)(2,1)} %collective-permute-done.6), channel_id=1, source_target_pairs={{0,4},{4,0},{8,12},{12,8},{1,5},{5,1},{9,13},{13,9},{2,6},{6,2},{1... | collective-permute-start | bytes 1572872 | tf_op jit(solution)/shard_map/ppermute | solution.py:10
  45.8 13.4 %collective-permute-start.5 = (bf16[1024,256]{1,0:T(8,128)(2,1)}, bf16[1024,256]{1,0:T(8,128)(2,1)}, u32[]{:S(2)}, u32[]{:S(2)}) collective-permute-start(bf16[1024,256]{1,0:T(8,128)(2,1)} %collective-permute-done.3), channel_id=1, source_target_pairs={{0,4},{4,0},{8,12},{12,8},{1,5},{5,1},{9,13},{13,9},{2,6},{6,2},{1... | collective-permute-start | bytes 1572872 | tf_op jit(solution)/shard_map/ppermute | solution.py:10
  54.3 5.0 %collective-permute-start.9 = (bf16[256,1024]{1,0:T(8,128)(2,1)}, bf16[256,1024]{1,0:T(8,128)(2,1)}, u32[]{:S(2)}, u32[]{:S(2)}) collective-permute-start(bf16[256,1024]{1,0:T(8,128)(2,1)} %collective-permute-done.7), channel_id=1, source_target_pairs={{0,4},{4,0},{8,12},{12,8},{1,5},{5,1},{9,13},{13,9},{2,6},{6,2},{1... | collective-permute-start | bytes 1572872 | tf_op jit(solution)/shard_map/ppermute | solution.py:10
  67.5 10.6 %collective-permute-start.12 = (bf16[128,1024]{1,0:T(8,128)(2,1)}, bf16[128,1024]{1,0:T(8,128)(2,1)}, u32[]{:S(2)}, u32[]{:S(2)}) collective-permute-start(bf16[128,1024]{1,0:T(8,128)(2,1)} %get-tuple-element.29), channel_id=1, source_target_pairs={{0,3},{1,0},{2,1},{3,2},{4,7},{5,4},{6,5},{7,6},{8,11},{9,8},{10,9... | collective-permute-start | bytes 786440 | tf_op jit(solution)/shard_map/ppermute | solution.py:124
  71.1 23.3 %collective-permute-start.11 = (bf16[128,1024]{1,0:T(8,128)(2,1)S(1)}, bf16[128,1024]{1,0:T(8,128)(2,1)}, u32[]{:S(2)}, u32[]{:S(2)}) collective-permute-start(bf16[128,1024]{1,0:T(8,128)(2,1)S(1)} %get-tuple-element.30), channel_id=1, source_target_pairs={{0,2},{1,3},{2,0},{3,1},{4,6},{5,7},{6,4},{7,5},{8,10},{9,11},{10,... | collective-permute-start | bytes 786440 | tf_op jit(solution)/shard_map/ppermute | solution.py:124
  71.1 23.3 %collective-permute-start.10 = (bf16[128,1024]{1,0:T(8,128)(2,1)S(1)}, bf16[128,1024]{1,0:T(8,128)(2,1)}, u32[]{:S(2)}, u32[]{:S(2)}) collective-permute-start(bf16[128,1024]{1,0:T(8,128)(2,1)S(1)} %get-tuple-element.28), channel_id=1, source_target_pairs={{0,1},{1,2},{2,3},{3,0},{4,5},{5,6},{6,7},{7,4},{8,9},{9,10},{10,1... | collective-permute-start | bytes 786440 | tf_op jit(solution)/shard_map/ppermute | solution.py:124
  72.2 38.8 %copy-start.4 = (bf16[1024,128]{1,0:T(8,128)(2,1)S(1)}, bf16[1024,128]{1,0:T(8,128)(2,1)}, u32[]{:S(2)}) copy-start(bf16[1024,128]{1,0:T(8,128)(2,1)} %param.15) | copy-start | bytes 786436
  72.2 38.8 %copy-start.5 = (f32[1024]{0:T(1024)S(1)}, f32[1024]{0:T(1024)}, u32[]{:S(2)}) copy-start(f32[1024]{0:T(1024)} %param.14) | copy-start | bytes 12292
  110.9 1.0 copy-start.6
Sparse Core Ops, SparseCore 0:
  11.5 33.1 all-gather.1
where the time goes:
time: 119 us
  waiting for transfers between devices  55.4 us (47%)
  blocking collectives  14.5 us (12%)
  between operations  14.3 us (12%)
  starting transfers between devices  12.9 us (11%)
  matrix products  12.5 us (11%)
  other arithmetic  7.9 us (7%)
  local copies, waits for them, and re-layouts  1.27 us (1%)
    ppermute x3, waiting for transfers between devices, local(): lax.ppermute(slice_for((tp_here + shift) % n_tp).astype(PARTIAL_DTYPE), '...  22.3 us
    ppermute x2, waiting for transfers between devices, from_chip_behind(): lax.ppermute(value, axis, [(i, (i + 2 * chips_back) % size) for i in rang...  22 us
    all_to_all x1, blocking collectives, local(): lax.all_to_all(jnp.concatenate([packed, spot_lanes], axis=1).reshape(n_de...  14.5 us
    dot_general x2, matrix products, apply_block(): return jnp.dot(hidden, down_here, preferred_element_type=jnp.float32)  10.9 us
    ppermute x2, waiting for transfers between devices, swap_parts(): lax.ppermute(value, 'rep', [(i, (i + step) % n_rep) for i in range(n_rep)])  7.94 us
    ppermute x2, starting transfers between devices, from_chip_behind(): lax.ppermute(value, axis, [(i, (i + 2 * chips_back) % size) for i in rang...  4.84 us
    ppermute x3, starting transfers between devices, local(): lax.ppermute(slice_for((tp_here + shift) % n_tp).astype(PARTIAL_DTYPE), '...  4.61 us
    all_gather x1, waiting for transfers between devices, local(): lax.all_gather(jnp.concatenate([normed, member_lanes], axis=1), 'tp', axi...  3.1 us
  transfers between devices with their start and end apart: 14, of which 6 were waited for; matrix products, arithmetic and copies ran while one was open for 5% of the time, Pallas kernels for 0%

commit v1 on v0

--- a/solution.py
+++ b/solution.py
@@ -1,9 +1,40 @@
+import functools
 import jax
 import jax.numpy as jnp
 from jax import lax
 from jax.sharding import PartitionSpec as P
+from jax.lax import axis_index, axis_size, ppermute
 
 PARTIAL_DTYPE = jnp.bfloat16
+
+
+def link_arrays(x_in, in_dim):
+    raw_out = axis_size("tp")
+    outcome_arr, block_next, current_arr = (raw_out, axis_index("tp"), x_in.shape[in_dim])
+    tray = tuple((c * outcome_arr if d == in_dim else c for d, c in enumerate(x_in.shape)))
+    built = jnp.zeros(tray, x_in.dtype)
+    far_arr = lax.dynamic_update_slice_in_dim(built, x_in, block_next * current_arr, axis=in_dim)
+    answer = latest = x_in
+    j = 1
+    while j < outcome_arr // 2 + 1:
+        answer = ppermute(
+            answer, "tp", tuple(((d, (d + 1) % outcome_arr) for d in range(outcome_arr)))
+        )
+        far_arr = lax.dynamic_update_slice_in_dim(
+            far_arr, answer, (block_next - j) % outcome_arr * current_arr, axis=in_dim
+        )
+        if 2 * j < outcome_arr:
+            latest = ppermute(
+                latest, "tp", tuple(((d, (d - 1) % outcome_arr) for d in range(outcome_arr)))
+            )
+            far_arr = lax.dynamic_update_slice_in_dim(
+                far_arr, latest, (block_next + j) % outcome_arr * current_arr, axis=in_dim
+            )
+        j = j + 1
+    return far_arr
+
+
+assign_limits = functools.partial(link_arrays, in_dim=0)
 
 
 def from_partner(value, axis, distance):
@@ -80,9 +111,7 @@
     member_lanes = jnp.where(
         jnp.arange(128, dtype=jnp.int32)[None, :] == 0, member[:, None], 0
     ).astype(jnp.bfloat16)
-    gathered = lax.all_gather(
-        jnp.concatenate([normed, member_lanes], axis=1), "tp", axis=0, tiled=True
-    )
+    gathered = assign_limits(jnp.concatenate([normed, member_lanes], axis=1))
     gathered_rows = gathered[:, :feature_width]
     gathered_member = gathered[:, feature_width].astype(jnp.int32)
 

time: 119 us -> 116 us (0.975)
  between operations: 14.3 us -> 1.06 us
  local copies, waits for them, and re-layouts: 1.27 us -> 7.47 us
  starting transfers between devices: 12.9 us -> 18 us
  other arithmetic: 7.9 us -> 4.77 us
  blocking collectives: 14.5 us -> 16.2 us
    ppermute x2, waiting for transfers between devices: 22 us -> 7.06 us  [from_chip_behind(): lax.ppermute(value, axis, [(i, (i + 2 * chips_back) % size) for i in rang...]
    ppermute x0 -> x3, waiting for transfers between devices: none -> 9.83 us  [the longest x1 6.26 us: link_arrays(): ppermute(latest, 'tp', tuple(((d, (d - 1) % outcome_arr) for d in range(o...]
    ppermute x2, waiting for transfers between devices: 7.94 us -> 17.2 us  [swap_parts(): lax.ppermute(value, 'rep', [(i, (i + step) % n_rep) for i in range(n_rep)])]
    ppermute x0 -> x3, starting transfers between devices: none -> 5.29 us  [the longest x1 3.6 us: link_arrays(): ppermute(latest, 'tp', tuple(((d, (d - 1) % outcome_arr) for d in range(o...]
    all_gather x1 -> x0, waiting for transfers between devices: 3.1 us -> none  [local(): lax.all_gather(jnp.concatenate([normed, member_lanes], axis=1), 'tp', axi...]
    dot_general x0 -> x1, matrix products: none -> 3.1 us  [apply_block(): jnp.dot(gathered_rows, up_here, preferred_element_type=jnp.float32)]
    dot_general x2, matrix products: 10.9 us -> 8.09 us  [apply_block(): return jnp.dot(hidden, down_here, preferred_element_type=jnp.float32)]
    ppermute x0 -> x3, local copies, waits for them, and re-layouts: none -> 2.54 us  [the longest x2 1.38 us: link_arrays(): ppermute(answer, 'tp', tuple(((d, (d + 1) % outcome_arr) for d in range(o...]
  transfers between devices with their start and end apart: 14 -> 16, of which waited for: 6 -> 7; matrix products, arithmetic and copies ran while one was open for 5% -> 11% of each run, Pallas kernels for 0% -> 0%
where the time goes in v1:
time: 116 us; the launch traced here: 115 us
  waiting for transfers between devices  55 us (47%)
  starting transfers between devices  18 us (16%)
  blocking collectives  16.2 us (14%)
  matrix products  12.7 us (11%)
  local copies, waits for them, and re-layouts  7.47 us (6%)
  other arithmetic  4.77 us (4%)
    ppermute x3, waiting for transfers between devices, local(): lax.ppermute(slice_for((tp_here + shift) % n_tp).astype(PARTIAL_DTYPE), '...  20.9 us
    ppermute x2, waiting for transfers between devices, swap_parts(): lax.ppermute(value, 'rep', [(i, (i + step) % n_rep) for i in range(n_rep)])  17.2 us
    all_to_all x1, blocking collectives, local(): lax.all_to_all(jnp.concatenate([packed, spot_lanes], axis=1).reshape(n_de...  16.2 us
    dot_general x2, matrix products, apply_block(): return jnp.dot(hidden, down_here, preferred_element_type=jnp.float32)  8.09 us
    ppermute x2, waiting for transfers between devices, from_chip_behind(): lax.ppermute(value, axis, [(i, (i + 2 * chips_back) % size) for i in rang...  7.06 us
    ppermute x1, waiting for transfers between devices, link_arrays(): ppermute(latest, 'tp', tuple(((d, (d - 1) % outcome_arr) for d in range(o...  6.26 us
    ppermute x3, starting transfers between devices, local(): lax.ppermute(slice_for((tp_here + shift) % n_tp).astype(PARTIAL_DTYPE), '...  4.95 us
    ppermute x2, starting transfers between devices, from_chip_behind(): lax.ppermute(value, axis, [(i, (i + 2 * chips_back) % size) for i in rang...  4.84 us
  transfers between devices with their start and end apart: 16, of which 7 were waited for; matrix products, arithmetic and copies ran while one was open for 11% of the time, Pallas kernels for 0%

profile of v1, /device:TPU:0, one launch (start us, length us, event | category | flops | bytes accessed | tf_op | source)
XLA Modules:
  0.0 115.2 jit_solution(17275557341946204100)
XLA Ops:
  0.7 1.1 dynamic-slice_bitcast_fusion
  1.8 3.0 %collective-permute-start.5 = (bf16[1024,256]{1,0:T(8,128)(2,1)S(1)}, bf16[1024,256]{1,0:T(8,128)(2,1)}, u32[]{:S(2)}, u32[]{:S(2)}) collective-permute-start(bf16[1024,256]{1,0:T(8,128)(2,1)S(1)} %dynamic-slice_bitcast_fusion), channel_id=1, source_target_pairs={{0,8},{4,12},{8,0},{12,4},{1,9},{5,13},{9,1},{13,5},{2,10},{6,14},... | collective-permute-start | bytes 1572872 | tf_op jit(solution)/shard_map/ppermute | solution.py:46
  4.8 0.7 and_select_fusion
  5.9 0.8 select_reduce_fusion.1
  7.2 0.8 gather_fusion
  8.2 1.6 %collective-permute-start = (bf16[128,1152]{1,0:T(8,128)(2,1)S(1)}, bf16[128,1152]{1,0:T(8,128)(2,1)S(1)}, u32[]{:S(2)}, u32[]{:S(2)}) collective-permute-start(bf16[128,1152]{1,0:T(8,128)(2,1)S(1)} %pad_maximum_fusion), channel_id=1, source_target_pairs={{0,1},{1,2},{2,3},{3,0},{4,5},{5,6},{6,7},{7,4},{8,9},{9,10},{10,1... | collective-permute-start | bytes 884744 | tf_op jit(solution)/shard_map/ppermute | solution.py:20
  9.8 7.1 %collective-permute-done.5 = bf16[1024,256]{1,0:T(8,128)(2,1)} collective-permute-done((bf16[1024,256]{1,0:T(8,128)(2,1)S(1)}, bf16[1024,256]{1,0:T(8,128)(2,1)}, u32[]{:S(2)}, u32[]{:S(2)}) %collective-permute-start.5) | collective-permute-done | bytes 524320 | tf_op jit(solution)/shard_map/ppermute | solution.py:46
  16.8 1.1 constant_dynamic-slice_fusion
  17.9 1.8 %collective-permute-start.9 = (bf16[256,1024]{1,0:T(8,128)(2,1)S(1)}, bf16[256,1024]{1,0:T(8,128)(2,1)}, u32[]{:S(2)}, u32[]{:S(2)}) collective-permute-start(bf16[256,1024]{1,0:T(8,128)(2,1)S(1)} %constant_dynamic-slice_fusion), channel_id=1, source_target_pairs={{0,8},{4,12},{8,0},{12,4},{1,9},{5,13},{9,1},{13,5},{2,10},{6,14},... | collective-permute-start | bytes 1572872 | tf_op jit(solution)/shard_map/ppermute | solution.py:46
  19.7 3.6 %collective-permute-start.1 = (bf16[128,1152]{1,0:T(8,128)(2,1)S(1)}, bf16[128,1152]{1,0:T(8,128)(2,1)}, u32[]{:S(2)}, u32[]{:S(2)}) collective-permute-start(bf16[128,1152]{1,0:T(8,128)(2,1)S(1)} %pad_maximum_fusion), channel_id=1, source_target_pairs={{0,3},{1,0},{2,1},{3,2},{4,7},{5,4},{6,5},{7,6},{8,11},{9,8},{10,9... | collective-permute-start | bytes 884744 | tf_op jit(solution)/shard_map/ppermute | solution.py:27
  24.4 6.3 %collective-permute-done.1 = bf16[128,1152]{1,0:T(8,128)(2,1)} collective-permute-done((bf16[128,1152]{1,0:T(8,128)(2,1)S(1)}, bf16[128,1152]{1,0:T(8,128)(2,1)}, u32[]{:S(2)}, u32[]{:S(2)}) %collective-permute-start.1) | collective-permute-done | bytes 294944 | tf_op jit(solution)/shard_map/ppermute | solution.py:27
  30.7 1.2 %copy.17 = bf16[128,1152]{0,1:T(8,128)(2,1)S(1)} copy(bf16[128,1152]{1,0:T(8,128)(2,1)} %collective-permute-done.1) | data formatting | bytes 589824 | tf_op jit(solution)/shard_map/ppermute | solution.py:27
  31.9 1.6 %collective-permute-start.6 = (bf16[1024,256]{1,0:T(8,128)(2,1)}, bf16[1024,256]{1,0:T(8,128)(2,1)}, u32[]{:S(2)}, u32[]{:S(2)}) collective-permute-start(bf16[1024,256]{1,0:T(8,128)(2,1)} %collective-permute-done.5), channel_id=1, source_target_pairs={{0,16},{16,0},{1,17},{17,1},{2,18},{18,2},{3,19},{19,3},{4,20},{20... | collective-permute-start | bytes 1572872 | tf_op jit(solution)/shard_map/ppermute | solution.py:52
  33.4 0.5 collective-permute-start.10
  34.0 3.6 %collective-permute-done.2 = bf16[128,1152]{1,0:T(8,128)(2,1)} collective-permute-done((bf16[128,1152]{1,0:T(8,128)(2,1)S(1)}, bf16[128,1152]{1,0:T(8,128)(2,1)}, u32[]{:S(2)}, u32[]{:S(2)}) %collective-permute-start.2) | collective-permute-done | bytes 294944 | tf_op jit(solution)/shard_map/ppermute | solution.py:20
  37.6 1.2 %copy.18 = bf16[128,1152]{0,1:T(8,128)(2,1)S(1)} copy(bf16[128,1152]{1,0:T(8,128)(2,1)} %collective-permute-done.2) | data formatting | bytes 589824 | tf_op jit(solution)/shard_map/ppermute | solution.py:20
  38.9 0.6 collective-permute-start.11
  39.5 7.6 %collective-permute-done.6 = bf16[1024,256]{1,0:T(8,128)(2,1)} collective-permute-done((bf16[1024,256]{1,0:T(8,128)(2,1)}, bf16[1024,256]{1,0:T(8,128)(2,1)}, u32[]{:S(2)}, u32[]{:S(2)}) %collective-permute-start.6) | collective-permute-done | bytes 524320 | tf_op jit(solution)/shard_map/ppermute | solution.py:52
  47.1 9.5 %collective-permute-done.10 = bf16[256,1024]{1,0:T(8,128)(2,1)} collective-permute-done((bf16[256,1024]{1,0:T(8,128)(2,1)}, bf16[256,1024]{1,0:T(8,128)(2,1)}, u32[]{:S(2)}, u32[]{:S(2)}) %collective-permute-start.10) | collective-permute-done | bytes 524320 | tf_op jit(solution)/shard_map/ppermute | solution.py:52
  56.7 5.1 %fusion.20 = f32[512,1024]{1,0:T(8,128)S(1)} fusion(bf16[512,1024]{1,0:T(8,128)(2,1)} %collective-permute-done.4, bf16[512,1024]{1,0:T(8,128)(2,1)} %bitcast.4, bf16[1024,512]{1,0:T(8,128)(2,1)} %collective-permute-done.3, bf16[1024,512]{1,0:T(8,128)(2,1)} %bitcast.3, bf16[512,1152]{0,1:T(8,128)(2,1)} %copy-done.3, bf16[512]{0:T(512)(128)(2,1)S(1)} %get-tuple-element.25), kind=kOutput, calls=%fused_computation.23 | convolution fusion | flops 2161115136 | bytes 7341056 | tf_op jit(solution)/shard_map/dot_general | solution.py:126
  61.8 3.1 %fusion.24 = f32[512,1024]{1,0:T(8,128)S(1)} fusion(bf16[1024,256]{1,0:T(8,128)(2,1)} %collective-permute-done.8, bf16[1024,256]{1,0:T(8,128)(2,1)} %collective-permute-done.7, bf16[1024,256]{1,0:T(8,128)(2,1)} %collective-permute-done.6, bf16[1024,256]{1,0:T(8,128)(2,1)} %collective-permute-done.5, bf16[512,1152]{0,1:T(8,128)(2,1)} %copy-done.3), kind=kOutput, calls=%fused_computation.27 | convolution fusion | flops 1082130432 | bytes 5242880 | tf_op jit(solution)/shard_map/dot_general | solution.py:121
  64.9 3.0 %fusion.32 = f32[512,1024]{1,0:T(8,128)S(1)} fusion(bf16[256,1024]{1,0:T(8,128)(2,1)} %collective-permute-done.12, bf16[256,1024]{1,0:T(8,128)(2,1)} %collective-permute-done.11, bf16[256,1024]{1,0:T(8,128)(2,1)} %collective-permute-done.10, bf16[256,1024]{1,0:T(8,128)(2,1)} %collective-permute-done.9, f32[512,1024]{1,0:T(8,128)S(1)} %fusion.24, ...), kind=kOutput, calls=%fused_computation.35 | convolution fusion | flops 1087373312 | bytes 6292480 | tf_op jit(solution)/shard_map/dot_general | solution.py:126
  67.9 1.3 %copy-done.2 = f32[512,1024]{1,0:T(8,128)} copy-done((f32[512,1024]{1,0:T(8,128)}, f32[512,1024]{1,0:T(8,128)S(1)}, u32[]{:S(2)}) %copy-start.2) | copy-done | bytes 2097176
  69.2 1.0 fusion.67
  70.2 4.4 %collective-permute-start.15 = (bf16[128,1024]{1,0:T(8,128)(2,1)}, bf16[128,1024]{1,0:T(8,128)(2,1)}, u32[]{:S(2)}, u32[]{:S(2)}) collective-permute-start(bf16[128,1024]{1,0:T(8,128)(2,1)} %get-tuple-element.29), channel_id=1, source_target_pairs={{0,3},{1,0},{2,1},{3,2},{4,7},{5,4},{6,5},{7,6},{8,11},{9,8},{10,9... | collective-permute-start | bytes 786440 | tf_op jit(solution)/shard_map/ppermute | solution.py:153
  74.6 0.6 collective-permute-start.13
  75.2 6.5 %collective-permute-done.15 = bf16[128,1024]{1,0:T(8,128)(2,1)} collective-permute-done((bf16[128,1024]{1,0:T(8,128)(2,1)}, bf16[128,1024]{1,0:T(8,128)(2,1)}, u32[]{:S(2)}, u32[]{:S(2)}) %collective-permute-start.15) | collective-permute-done | bytes 262176 | tf_op jit(solution)/shard_map/ppermute | solution.py:153
  81.6 14.4 %collective-permute-done.14 = bf16[128,1024]{1,0:T(8,128)(2,1)} collective-permute-done((bf16[128,1024]{1,0:T(8,128)(2,1)S(1)}, bf16[128,1024]{1,0:T(8,128)(2,1)}, u32[]{:S(2)}, u32[]{:S(2)}) %collective-permute-start.14) | collective-permute-done | bytes 262176 | tf_op jit(solution)/shard_map/ppermute | solution.py:153
  96.0 1.5 %fusion.64 = bf16[128,1024]{1,0:T(8,128)(2,1)S(1)} fusion(f32[128,1024]{1,0:T(8,128)S(1)} %get-tuple-element.36, bf16[128,1024]{1,0:T(8,128)(2,1)} %collective-permute-done.15, bf16[128,1024]{1,0:T(8,128)(2,1)} %collective-permute-done.14, bf16[128,1024]{1,0:T(8,128)(2,1)} %collective-permute-done.13, f32[4,128,1024]{2,1,0:T(8,128)} %bitcast.35, ...), kind=kLoop, calls=%fused_computation.64 | loop fusion | flops 1179648 | bytes 2621444 | tf_op jit(solution)/shard_map/convert_element_type | solution.py:158
  97.6 16.2 %all_to_all.5 = bf16[16,8,1152]{2,1,0:T(8,128)(2,1)S(1)} all-to-all(bf16[16,8,1152]{2,1,0:T(8,128)(2,1)S(1)} %maximum_bitcast_fusion), channel_id=1, replica_groups=mesh['rep'=2,'member'=4,'tp'=4] {'member','tp'}, dimensions={0} | all-to-all | bytes 589824 | tf_op jit(solution)/shard_map/all_to_all | solution.py:162
  113.9 0.3 fusion.58
  114.2 0.9 fusion.41
  (52 shorter events, 2.3 us)
Async XLA Ops:
  0.6 6.1 %copy-start = (bf16[128,1024]{1,0:T(8,128)(2,1)S(1)}, bf16[128,1024]{1,0:T(8,128)(2,1)}, u32[]{:S(2)}) copy-start(bf16[128,1024]{1,0:T(8,128)(2,1)} %param.8) | copy-start | bytes 786436
  0.6 6.5 %copy-start.1 = (f32[2,1024]{1,0:T(2,128)S(1)}, f32[2,1024]{1,0:T(2,128)}, u32[]{:S(2)}) copy-start(f32[2,1024]{1,0:T(2,128)} %param.11) | copy-start | bytes 24580
  1.8 15.1 %collective-permute-start.5 = (bf16[1024,256]{1,0:T(8,128)(2,1)S(1)}, bf16[1024,256]{1,0:T(8,128)(2,1)}, u32[]{:S(2)}, u32[]{:S(2)}) collective-permute-start(bf16[1024,256]{1,0:T(8,128)(2,1)S(1)} %dynamic-slice_bitcast_fusion), channel_id=1, source_target_pairs={{0,8},{4,12},{8,0},{12,4},{1,9},{5,13},{9,1},{13,5},{2,10},{6,14},... | collective-permute-start | bytes 1572872 | tf_op jit(solution)/shard_map/ppermute | solution.py:46
  8.2 15.9 %collective-permute-start = (bf16[128,1152]{1,0:T(8,128)(2,1)S(1)}, bf16[128,1152]{1,0:T(8,128)(2,1)S(1)}, u32[]{:S(2)}, u32[]{:S(2)}) collective-permute-start(bf16[128,1152]{1,0:T(8,128)(2,1)S(1)} %pad_maximum_fusion), channel_id=1, source_target_pairs={{0,1},{1,2},{2,3},{3,0},{4,5},{5,6},{6,7},{7,4},{8,9},{9,10},{10,1... | collective-permute-start | bytes 884744 | tf_op jit(solution)/shard_map/ppermute | solution.py:20
  17.9 15.5 %collective-permute-start.9 = (bf16[256,1024]{1,0:T(8,128)(2,1)S(1)}, bf16[256,1024]{1,0:T(8,128)(2,1)}, u32[]{:S(2)}, u32[]{:S(2)}) collective-permute-start(bf16[256,1024]{1,0:T(8,128)(2,1)S(1)} %constant_dynamic-slice_fusion), channel_id=1, source_target_pairs={{0,8},{4,12},{8,0},{12,4},{1,9},{5,13},{9,1},{13,5},{2,10},{6,14},... | collective-permute-start | bytes 1572872 | tf_op jit(solution)/shard_map/ppermute | solution.py:46
  19.7 19.2 %collective-permute-start.4 = (bf16[512,1024]{1,0:T(8,128)(2,1)}, bf16[512,1024]{1,0:T(8,128)(2,1)}, u32[]{:S(2)}, u32[]{:S(2)}) collective-permute-start(bf16[512,1024]{1,0:T(8,128)(2,1)} %bitcast.4), channel_id=1, source_target_pairs={{0,4},{4,0},{8,12},{12,8},{1,5},{5,1},{9,13},{13,9},{2,6},{6,2},{1... | collective-permute-start | bytes 3145736 | tf_op jit(solution)/shard_map/ppermute | solution.py:41
  19.7 11.0 %collective-permute-start.1 = (bf16[128,1152]{1,0:T(8,128)(2,1)S(1)}, bf16[128,1152]{1,0:T(8,128)(2,1)}, u32[]{:S(2)}, u32[]{:S(2)}) collective-permute-start(bf16[128,1152]{1,0:T(8,128)(2,1)S(1)} %pad_maximum_fusion), channel_id=1, source_target_pairs={{0,3},{1,0},{2,1},{3,2},{4,7},{5,4},{6,5},{7,6},{8,11},{9,8},{10,9... | collective-permute-start | bytes 884744 | tf_op jit(solution)/shard_map/ppermute | solution.py:27
  23.3 33.3 %collective-permute-start.3 = (bf16[1024,512]{1,0:T(8,128)(2,1)}, bf16[1024,512]{1,0:T(8,128)(2,1)}, u32[]{:S(2)}, u32[]{:S(2)}) collective-permute-start(bf16[1024,512]{1,0:T(8,128)(2,1)} %bitcast.3), channel_id=1, source_target_pairs={{0,4},{4,0},{8,12},{12,8},{1,5},{5,1},{9,13},{13,9},{2,6},{6,2},{1... | collective-permute-start | bytes 3145736 | tf_op jit(solution)/shard_map/ppermute | solution.py:41
  24.3 13.3 %collective-permute-start.2 = (bf16[128,1152]{1,0:T(8,128)(2,1)S(1)}, bf16[128,1152]{1,0:T(8,128)(2,1)}, u32[]{:S(2)}, u32[]{:S(2)}) collective-permute-start(bf16[128,1152]{1,0:T(8,128)(2,1)S(1)} %collective-permute-done), channel_id=1, source_target_pairs={{0,1},{1,2},{2,3},{3,0},{4,5},{5,6},{6,7},{7,4},{8,9},{9,10},{10,1... | collective-permute-start | bytes 884744 | tf_op jit(solution)/shard_map/ppermute | solution.py:20
  31.9 15.2 %collective-permute-start.6 = (bf16[1024,256]{1,0:T(8,128)(2,1)}, bf16[1024,256]{1,0:T(8,128)(2,1)}, u32[]{:S(2)}, u32[]{:S(2)}) collective-permute-start(bf16[1024,256]{1,0:T(8,128)(2,1)} %collective-permute-done.5), channel_id=1, source_target_pairs={{0,16},{16,0},{1,17},{17,1},{2,18},{18,2},{3,19},{19,3},{4,20},{20... | collective-permute-start | bytes 1572872 | tf_op jit(solution)/shard_map/ppermute | solution.py:52
  33.4 23.2 %collective-permute-start.10 = (bf16[256,1024]{1,0:T(8,128)(2,1)}, bf16[256,1024]{1,0:T(8,128)(2,1)}, u32[]{:S(2)}, u32[]{:S(2)}) collective-permute-start(bf16[256,1024]{1,0:T(8,128)(2,1)} %collective-permute-done.9), channel_id=1, source_target_pairs={{0,16},{16,0},{1,17},{17,1},{2,18},{18,2},{3,19},{19,3},{4,20},{20... | collective-permute-start | bytes 1572872 | tf_op jit(solution)/shard_map/ppermute | solution.py:52
  37.6 24.1 %collective-permute-start.7 = (bf16[1024,256]{1,0:T(8,128)(2,1)}, bf16[1024,256]{1,0:T(8,128)(2,1)}, u32[]{:S(2)}, u32[]{:S(2)}) collective-permute-start(bf16[1024,256]{1,0:T(8,128)(2,1)} %collective-permute-done.5), channel_id=1, source_target_pairs={{0,4},{4,0},{8,12},{12,8},{1,5},{5,1},{9,13},{13,9},{2,6},{6,2},{1... | collective-permute-start | bytes 1572872 | tf_op jit(solution)/shard_map/ppermute | solution.py:41
  38.9 17.8 %copy-start.3 = (bf16[512,1152]{0,1:T(8,128)(2,1)}, bf16[512,1152]{0,1:T(8,128)(2,1)S(1)}, u32[]{:S(2)}) copy-start(bf16[512,1152]{0,1:T(8,128)(2,1)S(1)} %constant_dynamic-update-slice_fusion) | copy-start | bytes 3538948
  38.9 22.8 %collective-permute-start.11 = (bf16[256,1024]{1,0:T(8,128)(2,1)}, bf16[256,1024]{1,0:T(8,128)(2,1)}, u32[]{:S(2)}, u32[]{:S(2)}) collective-permute-start(bf16[256,1024]{1,0:T(8,128)(2,1)} %collective-permute-done.9), channel_id=1, source_target_pairs={{0,4},{4,0},{8,12},{12,8},{1,5},{5,1},{9,13},{13,9},{2,6},{6,2},{1... | collective-permute-start | bytes 1572872 | tf_op jit(solution)/shard_map/ppermute | solution.py:41
  47.1 14.6 %collective-permute-start.8 = (bf16[1024,256]{1,0:T(8,128)(2,1)}, bf16[1024,256]{1,0:T(8,128)(2,1)}, u32[]{:S(2)}, u32[]{:S(2)}) collective-permute-start(bf16[1024,256]{1,0:T(8,128)(2,1)} %collective-permute-done.6), channel_id=1, source_target_pairs={{0,4},{4,0},{8,12},{12,8},{1,5},{5,1},{9,13},{13,9},{2,6},{6,2},{1... | collective-permute-start | bytes 1572872 | tf_op jit(solution)/shard_map/ppermute | solution.py:41
  56.7 5.1 %collective-permute-start.12 = (bf16[256,1024]{1,0:T(8,128)(2,1)}, bf16[256,1024]{1,0:T(8,128)(2,1)}, u32[]{:S(2)}, u32[]{:S(2)}) collective-permute-start(bf16[256,1024]{1,0:T(8,128)(2,1)} %collective-permute-done.10), channel_id=1, source_target_pairs={{0,4},{4,0},{8,12},{12,8},{1,5},{5,1},{9,13},{13,9},{2,6},{6,2},{1... | collective-permute-start | bytes 1572872 | tf_op jit(solution)/shard_map/ppermute | solution.py:41
  67.9 1.3 %copy-start.2 = (f32[512,1024]{1,0:T(8,128)}, f32[512,1024]{1,0:T(8,128)S(1)}, u32[]{:S(2)}) copy-start(f32[512,1024]{1,0:T(8,128)S(1)} %fusion.32) | copy-start | bytes 6291460
  70.2 11.4 %collective-permute-start.15 = (bf16[128,1024]{1,0:T(8,128)(2,1)}, bf16[128,1024]{1,0:T(8,128)(2,1)}, u32[]{:S(2)}, u32[]{:S(2)}) collective-permute-start(bf16[128,1024]{1,0:T(8,128)(2,1)} %get-tuple-element.29), channel_id=1, source_target_pairs={{0,3},{1,0},{2,1},{3,2},{4,7},{5,4},{6,5},{7,6},{8,11},{9,8},{10,9... | collective-permute-start | bytes 786440 | tf_op jit(solution)/shard_map/ppermute | solution.py:153
  74.6 21.4 %collective-permute-start.14 = (bf16[128,1024]{1,0:T(8,128)(2,1)S(1)}, bf16[128,1024]{1,0:T(8,128)(2,1)}, u32[]{:S(2)}, u32[]{:S(2)}) collective-permute-start(bf16[128,1024]{1,0:T(8,128)(2,1)S(1)} %get-tuple-element.30), channel_id=1, source_target_pairs={{0,2},{1,3},{2,0},{3,1},{4,6},{5,7},{6,4},{7,5},{8,10},{9,11},{10,... | collective-permute-start | bytes 786440 | tf_op jit(solution)/shard_map/ppermute | solution.py:153
  74.6 21.4 %collective-permute-start.13 = (bf16[128,1024]{1,0:T(8,128)(2,1)S(1)}, bf16[128,1024]{1,0:T(8,128)(2,1)}, u32[]{:S(2)}, u32[]{:S(2)}) collective-permute-start(bf16[128,1024]{1,0:T(8,128)(2,1)S(1)} %get-tuple-element.28), channel_id=1, source_target_pairs={{0,1},{1,2},{2,3},{3,0},{4,5},{5,6},{6,7},{7,4},{8,9},{9,10},{10,1... | collective-permute-start | bytes 786440 | tf_op jit(solution)/shard_map/ppermute | solution.py:153
  75.1 39.1 %copy-start.4 = (bf16[1024,128]{1,0:T(8,128)(2,1)S(1)}, bf16[1024,128]{1,0:T(8,128)(2,1)}, u32[]{:S(2)}) copy-start(bf16[1024,128]{1,0:T(8,128)(2,1)} %param.15) | copy-start | bytes 786436
  75.2 39.1 %copy-start.5 = (f32[1024]{0:T(1024)S(1)}, f32[1024]{0:T(1024)}, u32[]{:S(2)}) copy-start(f32[1024]{0:T(1024)} %param.14) | copy-start | bytes 12292
  114.2 1.0 copy-start.6
